TPU v7x, 128 devices: a whole 4x4x4 slice. The times are simulated.
128 devices in a mesh: req: 8 (over y, core), exp: 16 (over z, x).
Axes of the slice: x: 4, y: 4, z: 4, core: 2. Of those that a mesh axis runs over, the one named last changes fastest.
Arguments:
- hidden: bfloat16 [16384, 2560], P(('req', 'exp')), may hold values from -1.5 to 1.5
- queries: bfloat16 [16384, 1280], P(('req', 'exp')), may hold values from -100 to 100
- suffix_kv: bfloat16 [16384, 512], P(('req', 'exp')), may hold values from -24 to 24
- lengths: int32 [8, 4], P('req'), may hold values from 1 to 1024, 2048 in all within a row
- page_table: int32 [8, 4, 32], P('req'), may hold values from 0 to 55
- page_pool: bfloat16 [56, 128, 512], P('req'), may hold values from -24 to 24
- w_out: bfloat16 [1280, 2560], replicated, may hold values from -0.15625 to 0.15625
- w_router: bfloat16 [2560, 64], replicated, may hold values from -5 to 5
- routes: int32 [16384, 6], P(('req', 'exp')), may hold values from 0 to 63, all different within a row; in each aligned block of 128 rows (0 to 127, 128 to 255, ...) at most 15 rows name the same one
- w_gate: bfloat16 [128, 2560, 768], P(('req', 'exp')), may hold values from -0.125 to 0.125
- w_up: bfloat16 [128, 2560, 768], P(('req', 'exp')), may hold values from -0.125 to 0.125
- w_down: bfloat16 [128, 768, 2560], P(('req', 'exp')), may hold values from -0.4375 to 0.4375
Outputs:
- layer_out: bfloat16 [16384, 2560], P(('req', 'exp'))
Inputs may be any that keep to these rules, and one draw needn't show every extreme that they name: `lengths`: each row sums to 2048; its largest entry is exactly 1024. `page_table`: a page may appear in several prefixes and more than once in one. `routes`: the 6 experts of a token are distinct; among the rows of one device no expert is named more than 15 times, a bound that some block reaches.
All inputs are finite; a program needn't handle non-finite values.
Results may differ from a plain program's by a relative error of at most 0.022.
Values may be sent and summed in bfloat16 or wider, within the bound.
No kernel may reach another device: no remote copies, remote signals or barrier semaphores. Data moves between devices by JAX's collectives and lax.ppermute only.
A program may use at most 192 MiB of HBM per device.

v0:
```python
import math
import jax
import jax.numpy as jnp
from jax import lax
from jax.sharding import PartitionSpec as P

D = 2560
QUERY_HEADS = 10
KEY_VALUE_HEADS = 2
HEAD_SIZE = 128
TOP = 6
PAGE_TOKENS = 128
NEGATIVE_MASK = -1e30
EPS = 1e-06


def fold_scores(carry, query_matrix, key_rows, value_rows, weights):
    scores = jnp.einsum(
        "tgrd,kgd->tgrk", query_matrix, key_rows, preferred_element_type=jnp.float32
    ) * (1.0 / math.sqrt(HEAD_SIZE))
    running_maximum, grand_total, summed_output = carry
    live = weights[:, None, None, :] > 0
    fresh = jnp.maximum(running_maximum, jnp.max(jnp.where(live, scores, NEGATIVE_MASK), axis=-1))
    expo = jnp.where(live, jnp.exp(scores - fresh[..., None]), 0.0) * weights[:, None, None, :]
    decay = jnp.exp(running_maximum - fresh)
    grand_total = decay * grand_total + jnp.sum(expo, axis=-1)
    summed_output = decay[..., None] * summed_output + jnp.einsum(
        "tgrk,kgd->tgrd", expo.astype(jnp.bfloat16), value_rows, preferred_element_type=jnp.float32
    )
    return (fresh, grand_total, summed_output)


def empty_carry(token_count, request_groups):
    return (
        jnp.full((token_count, KEY_VALUE_HEADS, request_groups), NEGATIVE_MASK, jnp.float32),
        jnp.zeros((token_count, KEY_VALUE_HEADS, request_groups), jnp.float32),
        jnp.zeros((token_count, KEY_VALUE_HEADS, request_groups, HEAD_SIZE), jnp.float32),
    )


def on_device(
    hidden,
    queries,
    suffix_kv,
    lengths,
    page_table,
    page_pool,
    w_out,
    w_router,
    routes,
    w_gate,
    w_up,
    w_down,
):
    token_index = hidden.shape[0]
    row_width = KEY_VALUE_HEADS * HEAD_SIZE
    request_groups = QUERY_HEADS // KEY_VALUE_HEADS
    request_count = lax.axis_size("req")
    pool_per_shard = page_pool.shape[0]
    pool_all = pool_per_shard * request_count
    query_matrix = queries.reshape(token_index, KEY_VALUE_HEADS, request_groups, HEAD_SIZE)
    positions = lax.axis_index("exp") * token_index + jnp.arange(token_index, dtype=jnp.int32)
    lens = lengths[0]
    ends = jnp.cumsum(lens)
    starts = ends - lens
    req_of = jnp.sum((positions[:, None] >= ends[None, :]).astype(jnp.int32), axis=1)
    pick = req_of[:, None] == jnp.arange(lens.shape[0], dtype=jnp.int32)[None, :]
    first = jnp.sum(jnp.where(pick, starts[None, :], 0), axis=1)
    counts = jnp.sum(
        (page_table[0][:, :, None] == jnp.arange(pool_all, dtype=jnp.int32)[None, None, :]).astype(
            jnp.float32
        ),
        axis=1,
    )
    query_counts = jnp.dot(pick.astype(jnp.float32), counts, precision=lax.Precision.HIGHEST)
    query_total_set, every_count = (
        lax.all_gather(queries, "req", axis=0, tiled=True),
        lax.all_gather(query_counts.astype(jnp.bfloat16), "req", axis=0, tiled=True),
    )
    query_total_count = query_total_set.shape[0]
    local = lax.dynamic_slice_in_dim(
        every_count, lax.axis_index("req") * pool_per_shard, pool_per_shard, 1
    ).astype(jnp.float32)
    weights = jnp.repeat(local, PAGE_TOKENS, axis=1)
    flattened = page_pool.reshape(pool_per_shard * PAGE_TOKENS, 2 * row_width)
    key_rows = flattened[:, :row_width].reshape(
        pool_per_shard * PAGE_TOKENS, KEY_VALUE_HEADS, HEAD_SIZE
    )
    value_rows = flattened[:, row_width:].reshape(
        pool_per_shard * PAGE_TOKENS, KEY_VALUE_HEADS, HEAD_SIZE
    )
    running_maximum, grand_total, summed_output = fold_scores(
        empty_carry(query_total_count, request_groups),
        query_total_set.reshape(query_total_count, KEY_VALUE_HEADS, request_groups, HEAD_SIZE),
        key_rows,
        value_rows,
        weights,
    )
    peaks, totals, sums = (
        lax.all_to_all(
            running_maximum.reshape(request_count, token_index, KEY_VALUE_HEADS, request_groups),
            "req",
            split_axis=0,
            concat_axis=0,
            tiled=True,
        ),
        lax.all_to_all(
            grand_total.reshape(request_count, token_index, KEY_VALUE_HEADS, request_groups),
            "req",
            split_axis=0,
            concat_axis=0,
            tiled=True,
        ),
        lax.all_to_all(
            summed_output.reshape(
                request_count, token_index, KEY_VALUE_HEADS, request_groups, HEAD_SIZE
            ),
            "req",
            split_axis=0,
            concat_axis=0,
            tiled=True,
        ),
    )
    highest = jnp.max(peaks, axis=0)
    factor = jnp.exp(peaks - highest[None])
    carry = (highest, jnp.sum(factor * totals, axis=0), jnp.sum(factor[..., None] * sums, axis=0))
    segment = lax.all_gather(suffix_kv, "exp", axis=0, tiled=True)
    token_count = segment.shape[0]
    keypos = jnp.arange(token_count, dtype=jnp.int32)
    weights = (
        (keypos[None, :] <= positions[:, None]) & (keypos[None, :] >= first[:, None])
    ).astype(jnp.float32)
    key_rows = segment[:, :row_width].reshape(token_count, KEY_VALUE_HEADS, HEAD_SIZE)
    value_rows = segment[:, row_width:].reshape(token_count, KEY_VALUE_HEADS, HEAD_SIZE)
    running_maximum, grand_total, summed_output = fold_scores(
        carry, query_matrix, key_rows, value_rows, weights
    )
    attended = (
        (summed_output / grand_total[..., None])
        .reshape(token_index, QUERY_HEADS * HEAD_SIZE)
        .astype(jnp.bfloat16)
    )
    projected = jnp.dot(attended, w_out, preferred_element_type=jnp.float32)
    resid = lax.optimization_barrier((hidden.astype(jnp.float32) + projected).astype(jnp.bfloat16))
    resid_f = resid.astype(jnp.float32)
    normed = (resid_f * lax.rsqrt(jnp.mean(resid_f * resid_f, axis=1, keepdims=True) + EPS)).astype(
        jnp.bfloat16
    )
    n_experts = w_router.shape[1]
    logits = jnp.dot(normed, w_router, preferred_element_type=jnp.float32)
    expert_ids = jnp.arange(n_experts, dtype=jnp.int32)
    chosen = jnp.sum(
        jnp.where(routes[:, :, None] == expert_ids[None, None, :], logits[:, None, :], 0.0), axis=2
    )
    gates = jax.nn.softmax(chosen, axis=1)
    capacity = 16
    member = routes[:, :, None] == expert_ids[None, None, :]
    picks = jnp.any(member, axis=1).astype(jnp.float32)
    gate_of = jnp.sum(jnp.where(member, gates[:, :, None], 0.0), axis=1)
    earlier = (
        jnp.arange(token_index, dtype=jnp.int32)[:, None]
        > jnp.arange(token_index, dtype=jnp.int32)[None, :]
    ).astype(jnp.float32)
    rank = jnp.dot(earlier, picks, precision=lax.Precision.HIGHEST).astype(jnp.int32)
    place = jnp.arange(capacity, dtype=jnp.int32)
    select = (picks[None, :, :] > 0) & (rank[None, :, :] == place[:, None, None])
    select = jnp.transpose(select, (2, 0, 1))
    select2 = jnp.broadcast_to(select[:, None], (n_experts, 2, capacity, token_index)).reshape(
        2 * n_experts * capacity, token_index
    )
    outgoing = jnp.dot(
        select2.astype(jnp.bfloat16), normed, preferred_element_type=jnp.float32
    ).astype(jnp.bfloat16)
    outgoing = outgoing.reshape(2 * n_experts, capacity, D)
    rows = lax.all_to_all(outgoing, ("req", "exp"), split_axis=0, concat_axis=0, tiled=True)
    array_shape = rows.shape
    flat_rows = rows.reshape(-1, D)
    gate_part = jnp.dot(flat_rows, w_gate[0], preferred_element_type=jnp.float32)
    up_part = jnp.dot(flat_rows, w_up[0], preferred_element_type=jnp.float32)
    inner = (jax.nn.silu(gate_part) * up_part).astype(jnp.bfloat16)
    returned = lax.all_to_all(
        jnp.dot(inner, w_down[0], preferred_element_type=jnp.float32)
        .astype(jnp.bfloat16)
        .reshape(array_shape),
        ("req", "exp"),
        split_axis=0,
        concat_axis=0,
        tiled=True,
    ).reshape(2 * n_experts * capacity, D)
    weight = jnp.where(
        jnp.transpose(select, (2, 0, 1))[:, :, None, :], gate_of[:, :, None, None], 0.0
    )
    weight = jnp.broadcast_to(weight, (token_index, n_experts, 2, capacity)).reshape(
        token_index, 2 * n_experts * capacity
    )
    high = weight.astype(jnp.bfloat16)
    low = (weight - high.astype(jnp.float32)).astype(jnp.bfloat16)
    moe = jnp.dot(high, returned, preferred_element_type=jnp.float32) + jnp.dot(
        low, returned, preferred_element_type=jnp.float32
    )
    return (resid_f + moe).astype(jnp.bfloat16)


def solution(mesh):
    placed = (
        P(("req", "exp"), None),
        P(("req", "exp"), None),
        P(("req", "exp"), None),
        P("req", None),
        P("req", None, None),
        P("req", None, None),
        P(),
        P(),
        P(("req", "exp"), None),
        P(("req", "exp"), None, None),
        P(("req", "exp"), None, None),
        P(("req", "exp"), None, None),
    )
    return jax.shard_map(
        on_device, mesh=mesh, in_specs=placed, out_specs=P(("req", "exp"), None), check_vma=False
    )
```

profile of v0, /device:TPU:34, one launch (start us, length us, event | category | flops | bytes accessed | tf_op | source)
XLA Modules:
  0.0 531.8 jit_solution(14392213772407807917)
XLA Ops:
  11.2 12.1 %all_gather.9 = bf16[1024,56]{0,1:T(8,128)(2,1)S(1)} all-gather(bf16[128,56]{0,1:T(8,128)(2,1)S(1)} %convolution_convert_fusion.3), channel_id=1, replica_groups=mesh['req'=8,'exp'=16] {'req'}, dimensions={0}, use_global_device_ids=true | all-gather | bytes 129024 | tf_op jit(solution)/shard_map/all_gather | solution.py:78
  25.1 16.3 %all-gather.3.cloned.1.call-done = bf16[1024,1280]{0,1:T(8,128)(2,1)} async-done(((bf16[128,1280]{0,1:T(8,128)(2,1)}), bf16[1024,1280]{0,1:T(8,128)(2,1)}) %all-gather.3.cloned.1.call-update) | async-done | bytes 2621456 | tf_op jit(solution)/shard_map/all_gather | solution.py:77
  41.4 16.3 %fusion = (f32[1024,2,5]{0,2,1:T(8,128)S(1)}, f32[2,896,1024,5]{2,1,3,0:T(8,128)}) fusion(pred[1024,896]{0,1:T(8,128)(4,1)S(1)} %bitcast_compare_fusion, bf16[896,2,128,1]{0,2,3,1:T(8,128)(2,1)S(1)} %bitcast.144, bf16[1024,2,5,128]{0,3,2,1:T(8,128)(2,1)} %bitcast.138), kind=kOutput, calls=%fused_computation.2 | convolution fusion | flops 2376325120 | bytes 40738816 | tf_op jit(solution)/shard_map/tgrd,kgd->tgrk/dot_general | solution.py:18
  60.0 15.7 %fusion.4 = f32[1024,2,5]{0,2,1:T(8,128)S(1)} fusion(f32[2,896,1024,5]{2,1,3,0:T(8,128)} %get-tuple-element.20, f32[1024,896]{0,1:T(8,128)S(1)} %bitcast.133, f32[1024,2,5]{0,2,1:T(8,128)S(1)} %get-tuple-element.14, pred[1024,896]{0,1:T(8,128)(4,1)S(1)} %bitcast_compare_fusion), kind=kLoop, calls=%fused_computation.6 | loop fusion | flops 45864960 | bytes 41369600 | tf_op jit(solution)/shard_map/reduce_sum | solution.py:26
  76.3 4.0 all-to-all-start.2
  82.1 3.8 all-to-all-done.2
  85.8 3.3 all-to-all-start
  89.2 17.4 %bitcast_add_fusion = f32[1024,2,5,128]{3,0,2,1:T(8,128)S(1)} fusion(f32[1024,2,5]{0,2,1:T(8,128)S(1)} %get-tuple-element.13, bf16[896,2,128,1]{0,2,3,1:T(8,128)(2,1)S(1)} %bitcast.150, f32[2,896,1024,5]{2,1,3,0:T(8,128)} %get-tuple-element.20, f32[1024,896]{0,1:T(8,128)} %bitcast.134, f32[1024,2,5]{0,2,1:T(8,128)S(1)} %get-tuple-element.14, ...), kind=kOutput, calls=%fused_computation.21 | convolution fusion | flops 2395996160 | bytes 47071232 | tf_op jit(solution)/shard_map/tgrk,kgd->tgrd/dot_general | solution.py:27
  109.4 5.0 all-to-all-start.1
  115.1 15.4 %all-gather.5.cloned.1.call-done = bf16[2048,512]{0,1:T(8,128)(2,1)} async-done(((bf16[128,512]{0,1:T(8,128)(2,1)}), bf16[2048,512]{0,1:T(8,128)(2,1)}) %all-gather.5.cloned.1.call-update) | async-done | bytes 2097168 | tf_op jit(solution)/shard_map/all_gather | solution.py:127
  133.2 5.8 %fusion.9 = (f32[128,2,5]{0,2,1:T(8,128)S(1)}, f32[2,2048,128,5]{2,1,3,0:T(8,128)}) fusion(pred[128,2048]{0,1:T(8,128)(4,1)S(1)} %get-tuple-element.17, bf16[2048,2,128,1]{0,2,3,1:T(8,128)(2,1)S(1)} %bitcast.141, bf16[128,2,5,128]{0,3,2,1:T(8,128)(2,1)S(1)} %bitcast.140), kind=kOutput, calls=%fused_computation.14 | convolution fusion | flops 678951680 | bytes 12129280 | tf_op jit(solution)/shard_map/tgrd,kgd->tgrk/dot_general | solution.py:18
  139.2 6.4 %fusion.13 = f32[128,2,5]{0,2,1:T(8,128)S(1)} fusion(f32[2,2048,128,5]{2,1,3,0:T(8,128)} %get-tuple-element.22, f32[128,2048]{0,1:T(8,128)S(1)} %get-tuple-element.18, f32[128,2,5]{0,2,1:T(8,128)S(1)} %copy.161, pred[128,2048]{0,1:T(8,128)(4,1)S(1)} %get-tuple-element.17), kind=kLoop, calls=%fused_computation.18 | loop fusion | flops 13105920 | bytes 11806720 | tf_op jit(solution)/shard_map/reduce_sum | solution.py:26
  145.7 29.6 %all-to-all-done.1 = f32[8,128,2,5,128]{4,1,3,2,0:T(8,128)} async-done(((f32[8,128,2,5,128]{4,1,3,2,0:T(8,128)}), f32[8,128,2,5,128]{4,1,3,2,0:T(8,128)}, u32[]{:S(2)}, u32[]{:S(2)}) %all-to-all-start.1) | async-done | bytes 5242912 | tf_op jit(solution)/shard_map/all_to_all | solution.py:114
  175.3 4.3 multiply_reduce_fusion
  181.8 7.9 %fusion.42 = bf16[128,2,5,128]{0,3,2,1:T(8,128)(2,1)S(1)} fusion(bf16[2048,2,128,1]{0,2,3,1:T(8,128)(2,1)} %bitcast.147, f32[2,2048,128,5]{2,1,3,0:T(8,128)} %get-tuple-element.22, f32[128,2048]{0,1:T(8,128)} %copy-done.4, f32[128,2,5]{0,2,1:T(8,128)S(1)} %copy.161, pred[128,2048]{0,1:T(8,128)(4,1)S(1)} %get-tuple-element.17, ...), kind=kOutput, calls=%fused_computation.49 | convolution fusion | flops 684851200 | bytes 13843456 | tf_op jit(solution)/shard_map/tgrk,kgd->tgrd/dot_general | solution.py:27
  191.0 3.2 convolution_convert_fusion.1
  194.3 126.3 %all_to_all.25 = bf16[128,16,2560]{2,1,0:T(8,128)(2,1)S(1)} all-to-all(bf16[128,16,2560]{2,1,0:T(8,128)(2,1)S(1)} %bitcast.130), channel_id=1, replica_groups=mesh['req'=8,'exp'=16] {'req','exp'}, dimensions={0} | all-to-all | bytes 20971520 | tf_op jit(solution)/shard_map/all_to_all | solution.py:175
  320.5 3.8 copy-done.2
  324.4 10.2 %fusion.21 = f32[2048,768]{1,0:T(8,128)} fusion(bf16[2048,2560]{1,0:T(8,128)(2,1)S(1)} %bitcast.136, bf16[1,2560,768]{2,1,0:T(8,128)(2,1)S(1)} %copy-done.8), kind=kOutput, calls=%fused_computation.27 | convolution fusion | flops 8053063680 | bytes 20709376 | tf_op jit(solution)/shard_map/dot_general | solution.py:178
  334.5 28.9 %convolution_convert_fusion = bf16[2048,2560]{1,0:T(8,128)(2,1)} fusion(f32[2048,768]{1,0:T(8,128)} %fusion.21, bf16[2048,2560]{1,0:T(8,128)(2,1)} %bitcast.137, bf16[1,768,2560]{2,1,0:T(8,128)(2,1)} %param.23, bf16[1,2560,768]{2,1,0:T(8,128)(2,1)} %param.22), kind=kOutput, calls=%fused_computation.10 | convolution fusion | flops 16120807424 | bytes 35127296 | tf_op jit(solution)/shard_map/dot_general | solution.py:182
  363.5 6.7 %all-to-all-start.4 = ((bf16[128,16,2560]{2,1,0:T(8,128)(2,1)}), bf16[128,16,2560]{2,1,0:T(8,128)(2,1)}, u32[]{:S(2)}, u32[]{:S(2)}) async-start(bf16[128,16,2560]{2,1,0:T(8,128)(2,1)} %bitcast.135), calls=%async_computation.4 | async-start | bytes 20971520 | tf_op jit(solution)/shard_map/all_to_all | solution.py:181
  371.0 141.3 %all-to-all-done.4 = bf16[128,16,2560]{2,1,0:T(8,128)(2,1)} async-done(((bf16[128,16,2560]{2,1,0:T(8,128)(2,1)}), bf16[128,16,2560]{2,1,0:T(8,128)(2,1)}, u32[]{:S(2)}, u32[]{:S(2)}) %all-to-all-start.4) | async-done | bytes 10485792 | tf_op jit(solution)/shard_map/all_to_all | solution.py:181
  512.3 5.5 %fusion.70 = f32[128,2560]{1,0:T(8,128)S(1)} fusion(bf16[128,2048]{0,1:T(8,128)(2,1)S(1)} %bitcast.143, bf16[2048,2560]{1,0:T(8,128)(2,1)} %bitcast.34), kind=kOutput, calls=%fused_computation.101 | convolution fusion | flops 1342177280 | bytes 12320768 | tf_op jit(solution)/shard_map/dot_general | solution.py:198
  518.0 6.4 %fusion.24 = bf16[128,2560]{1,0:T(8,128)(2,1)} fusion(f32[128,2560]{1,0:T(8,128)S(1)} %fusion.70, bf16[128,2048]{0,1:T(8,128)(2,1)S(1)} %bitcast.142, bf16[2048,2560]{1,0:T(8,128)(2,1)} %bitcast.34, bf16[128,2560]{1,0:T(8,128)(2,1)S(1)} %fusion.25), kind=kOutput, calls=%fused_computation.32 | convolution fusion | flops 1343488000 | bytes 13631488 | tf_op jit(solution)/shard_map/dot_general | solution.py:198
  (81 shorter events, 21.0 us)
Async XLA Ops:
  7.4 362.8 %copy-start = (bf16[2560,64]{0,1:T(8,128)(2,1)S(1)}, bf16[2560,64]{0,1:T(8,128)(2,1)}, u32[]{:S(2)}) copy-start(bf16[2560,64]{0,1:T(8,128)(2,1)} %param.19) | copy-start | bytes 983044
  7.4 34.0 %all-gather.3.cloned.1.call-start = ((), (), s32[]{:S(2)}) async-start(), calls=%async_computation.5 | async-start | bytes 2949120 | tf_op jit(solution)/shard_map/all_gather | solution.py:77
  58.2 1.8 copy-start.1
  60.0 20.4 %copy-start.6 = (bf16[128,512]{1,0:T(8,128)(2,1)S(1)}, bf16[128,512]{1,0:T(8,128)(2,1)}, u32[]{:S(2)}) copy-start(bf16[128,512]{1,0:T(8,128)(2,1)} %param.14) | copy-start | bytes 393220
  76.3 9.5 %all-to-all-start.2 = ((f32[8,128,2,5]{1,2,3,0:T(2,128)}), f32[8,128,2,5]{1,2,3,0:T(2,128)S(1)}, u32[]{:S(2)}, u32[]{:S(2)}) async-start(f32[8,128,2,5]{1,2,3,0:T(2,128)} %copy.164), calls=%async_computation.2 | async-start | bytes 81920 | tf_op jit(solution)/shard_map/all_to_all | solution.py:107
  80.3 50.2 %all-gather.5.cloned.1.call-start = ((), (), s32[]{:S(2)}) async-start(), calls=%async_computation.6 | async-start | bytes 2228224 | tf_op jit(solution)/shard_map/all_gather | solution.py:127
  85.8 23.6 %all-to-all-start = ((f32[8,128,2,5]{1,2,3,0:T(2,128)}), f32[8,128,2,5]{1,2,3,0:T(2,128)S(1)}, u32[]{:S(2)}, u32[]{:S(2)}) async-start(f32[8,128,2,5]{1,2,3,0:T(2,128)} %copy.144), calls=%async_computation | async-start | bytes 81920 | tf_op jit(solution)/shard_map/all_to_all | solution.py:100
  106.6 7.7 %copy-start.9 = (s32[1,4]{1,0:T(1,128)S(1)}, s32[1,4]{1,0:T(1,128)}, u32[]{:S(2)}) copy-start(s32[1,4]{1,0:T(1,128)} %param.15) | copy-start | bytes 52
  106.6 7.8 %copy-start.7 = (s32[128,6]{0,1:T(8,128)S(1)}, s32[128,6]{0,1:T(8,128)}, u32[]{:S(2)}) copy-start(s32[128,6]{0,1:T(8,128)} %param.20) | copy-start | bytes 9220
  109.4 23.9 %copy-start.3 = (bf16[128,1280]{0,1:T(8,128)(2,1)S(1)}, bf16[128,1280]{0,1:T(8,128)(2,1)}, u32[]{:S(2)}) copy-start(bf16[128,1280]{0,1:T(8,128)(2,1)} %copy.140) | copy-start | bytes 983044
  109.4 65.9 %all-to-all-start.1 = ((f32[8,128,2,5,128]{4,1,3,2,0:T(8,128)}), f32[8,128,2,5,128]{4,1,3,2,0:T(8,128)}, u32[]{:S(2)}, u32[]{:S(2)}) async-start(f32[8,128,2,5,128]{4,1,3,2,0:T(8,128)} %copy.158), calls=%async_computation.1 | async-start | bytes 10485760 | tf_op jit(solution)/shard_map/all_to_all | solution.py:114
  115.1 24.1 %copy-start.4 = (f32[128,2048]{0,1:T(8,128)}, f32[128,2048]{0,1:T(8,128)S(1)}, u32[]{:S(2)}) copy-start(f32[128,2048]{0,1:T(8,128)S(1)} %get-tuple-element.18) | copy-start | bytes 3145732
  175.3 14.4 %slice-start = ((s8[6553600]{0:T(1024)(128)(4,1)}), s8[2359296]{0:T(1024)(128)(4,1)S(1)}, s32[]{:S(2)}) async-start(s8[6553600]{0:T(1024)(128)(4,1)} %bitcast.131), calls=%async_computation.7 | async-start | bytes 4718592
  181.8 7.9 %slice-start.1 = ((s8[6553600]{0:T(1024)(128)(4,1)}), s8[4194304]{0:T(1024)(128)(4,1)S(1)}, s32[]{:S(2)}) async-start(s8[6553600]{0:T(1024)(128)(4,1)} %bitcast.131), calls=%async_computation.8 | async-start | bytes 8388608
  181.8 7.9 %copy-start.5 = (bf16[128,2560]{1,0:T(8,128)(2,1)S(1)}, bf16[128,2560]{1,0:T(8,128)(2,1)}, u32[]{:S(2)}) copy-start(bf16[128,2560]{1,0:T(8,128)(2,1)} %param.12) | copy-start | bytes 1966084
  194.3 130.1 %copy-start.8 = (bf16[1,2560,768]{2,1,0:T(8,128)(2,1)S(1)}, bf16[1,2560,768]{2,1,0:T(8,128)(2,1)}, u32[]{:S(2)}) copy-start(bf16[1,2560,768]{2,1,0:T(8,128)(2,1)} %param.21) | copy-start | bytes 11796484
  320.5 3.8 copy-start.2
  363.5 148.8 %all-to-all-start.4 = ((bf16[128,16,2560]{2,1,0:T(8,128)(2,1)}), bf16[128,16,2560]{2,1,0:T(8,128)(2,1)}, u32[]{:S(2)}, u32[]{:S(2)}) async-start(bf16[128,16,2560]{2,1,0:T(8,128)(2,1)} %bitcast.135), calls=%async_computation.4 | async-start | bytes 20971520 | tf_op jit(solution)/shard_map/all_to_all | solution.py:181
Sparse Core Ops, SparseCore 0:
  9.9 31.4 all-gather.2
Sparse Core Ops, SparseCore 1:
  82.9 47.5 all-gather.4
where the time goes:
time: 533 us; the launch traced here: 532 us
  waiting for transfers between devices  206 us (39%)
  blocking collectives  138 us (26%)
  matrix products  104 us (20%)
  other arithmetic  29.7 us (6%)
  local copies, waits for them, and re-layouts  19.7 us (4%)
  starting transfers between devices  19 us (4%)
  between operations  15.2 us (3%)
    all_to_all x1, waiting for transfers between devices, on_device(): lax.all_to_all(jnp.dot(inner, w_down[0], preferred_element_type=jnp.float...  141 us
    all_to_all x1, blocking collectives, on_device(): lax.all_to_all(outgoing, ('req', 'exp'), split_axis=0, concat_axis=0, til...  126 us
    all_to_all x1, waiting for transfers between devices, on_device(): lax.all_to_all(summed_output.reshape(request_count, token_index, KEY_VALU...  29.6 us
    dot_general x1, matrix products, on_device(): jnp.dot(inner, w_down[0], preferred_element_type=jnp.float32)  28.9 us
    dot_general x2, matrix products, fold_scores(): jnp.einsum('tgrk,kgd->tgrd', expo.astype(jnp.bfloat16), value_rows, prefe...  25.3 us
    dot_general x2, matrix products, fold_scores(): jnp.einsum('tgrd,kgd->tgrk', query_matrix, key_rows, preferred_element_ty...  22.1 us
    reduce_sum x2, other arithmetic, fold_scores(): grand_total = decay * grand_total + jnp.sum(expo, axis=-1)  22.1 us
    all_gather x1, waiting for transfers between devices, on_device(): lax.all_gather(queries, 'req', axis=0, tiled=True)  16.3 us
  transfers between devices with their start and end apart: 6, of which 5 were waited for; matrix products, arithmetic and copies ran while one was open for 8% of the time, Pallas kernels for 0%

commit v1 on v0

--- a/solution.py
+++ b/solution.py
@@ -12,6 +12,27 @@
 PAGE_TOKENS = 128
 NEGATIVE_MASK = -1e30
 EPS = 1e-06
+
+
+def ring_gather(x, axis, dim):
+    length, index, extent = (lax.axis_size(axis), lax.axis_index(axis), x.shape[dim])
+    forward = [(i, (i + 1) % length) for i in range(length)]
+    backward = [(i, (i - 1) % length) for i in range(length)]
+    result = jnp.zeros((*x.shape[:dim], length * extent, *x.shape[dim + 1 :]), x.dtype)
+    result = lax.dynamic_update_slice_in_dim(result, x, index * extent, axis=dim)
+    from_left = from_right = x
+    middle = length // 2
+    for step in range(1, middle + 1):
+        from_left = lax.ppermute(from_left, axis, forward)
+        result = lax.dynamic_update_slice_in_dim(
+            result, from_left, (index - step) % length * extent, axis=dim
+        )
+        if step < length - middle:
+            from_right = lax.ppermute(from_right, axis, backward)
+            result = lax.dynamic_update_slice_in_dim(
+                result, from_right, (index + step) % length * extent, axis=dim
+            )
+    return result
 
 
 def fold_scores(carry, query_matrix, key_rows, value_rows, weights):
@@ -124,7 +145,7 @@
     highest = jnp.max(peaks, axis=0)
     factor = jnp.exp(peaks - highest[None])
     carry = (highest, jnp.sum(factor * totals, axis=0), jnp.sum(factor[..., None] * sums, axis=0))
-    segment = lax.all_gather(suffix_kv, "exp", axis=0, tiled=True)
+    segment = ring_gather(suffix_kv, "exp", 0)
     token_count = segment.shape[0]
     keypos = jnp.arange(token_count, dtype=jnp.int32)
     weights = (

time: 533 us -> 560 us (1.051); the launches traced: 532 us -> 551 us
  starting transfers between devices: 19 us -> 55.8 us
  waiting for transfers between devices: 206 us -> 178 us
  blocking collectives: 138 us -> 147 us
    all_to_all x1, waiting for transfers between devices: 29.6 us -> 0.01 us  [on_device(): lax.all_to_all(summed_output.reshape(request_count, token_index, KEY_VALU...]
    ppermute x0 -> x15, waiting for transfers between devices: none -> 24.8 us  [the longest x8 24.8 us: ring_gather(): from_left = lax.ppermute(from_left, axis, forward)]
    ppermute x0 -> x15, starting transfers between devices: none -> 23.2 us  [the longest x7 18.1 us: ring_gather(): from_right = lax.ppermute(from_right, axis, backward)]
    all_gather x1 -> x0, waiting for transfers between devices: 15.4 us -> none  [on_device(): segment = lax.all_gather(suffix_kv, 'exp', axis=0, tiled=True)]
    all_to_all x1, starting transfers between devices: 4.95 us -> 17 us  [on_device(): lax.all_to_all(summed_output.reshape(request_count, token_index, KEY_VALU...]
    all_to_all x1, blocking collectives: 126 us -> 134 us  [on_device(): lax.all_to_all(outgoing, ('req', 'exp'), split_axis=0, concat_axis=0, til...]
  transfers between devices with their start and end apart: 6 -> 20, of which waited for: 5 -> 9; matrix products, arithmetic and copies ran while one was open for 8% -> 14% of each run, Pallas kernels for 0% -> 0%
where the time goes in v1:
time: 560 us; the launch traced here: 551 us
  waiting for transfers between devices  178 us (32%)
  blocking collectives  147 us (26%)
  matrix products  104 us (19%)
  starting transfers between devices  55.8 us (10%)
  other arithmetic  30.9 us (6%)
  local copies, waits for them, and re-layouts  21.7 us (4%)
  between operations  14.6 us (3%)
    all_to_all x1, waiting for transfers between devices, on_device(): lax.all_to_all(jnp.dot(inner, w_down[0], preferred_element_type=jnp.float...  141 us
    all_to_all x1, blocking collectives, on_device(): lax.all_to_all(outgoing, ('req', 'exp'), split_axis=0, concat_axis=0, til...  134 us
    dot_general x1, matrix products, on_device(): jnp.dot(inner, w_down[0], preferred_element_type=jnp.float32)  28.9 us
    dot_general x2, matrix products, fold_scores(): jnp.einsum('tgrk,kgd->tgrd', expo.astype(jnp.bfloat16), value_rows, prefe...  25.5 us
    ppermute x8, waiting for transfers between devices, ring_gather(): from_left = lax.ppermute(from_left, axis, forward)  24.8 us
    dot_general x2, matrix products, fold_scores(): jnp.einsum('tgrd,kgd->tgrk', query_matrix, key_rows, preferred_element_ty...  22.1 us
    reduce_sum x2, other arithmetic, fold_scores(): grand_total = decay * grand_total + jnp.sum(expo, axis=-1)  22.1 us
    ppermute x7, starting transfers between devices, ring_gather(): from_right = lax.ppermute(from_right, axis, backward)  18.1 us
  transfers between devices with their start and end apart: 20, of which 9 were waited for; matrix products, arithmetic and copies ran while one was open for 14% of the time, Pallas kernels for 0%

profile of v1, /device:TPU:34, one launch (start us, length us, event | category | flops | bytes accessed | tf_op | source)
XLA Modules:
  0.0 550.8 jit_solution(1584624167168252355)
XLA Ops:
  13.5 12.1 %all_gather.6 = bf16[1024,56]{0,1:T(8,128)(2,1)S(1)} all-gather(bf16[128,56]{0,1:T(8,128)(2,1)S(1)} %convolution_convert_fusion.3), channel_id=1, replica_groups=mesh['req'=8,'exp'=16] {'req'}, dimensions={0}, use_global_device_ids=true | all-gather | bytes 129024 | tf_op jit(solution)/shard_map/all_gather | solution.py:99
  29.6 11.4 %all-gather.2.cloned.1.call-done = bf16[1024,1280]{0,1:T(8,128)(2,1)} async-done(((bf16[128,1280]{0,1:T(8,128)(2,1)}), bf16[1024,1280]{0,1:T(8,128)(2,1)}) %all-gather.2.cloned.1.call-update) | async-done | bytes 2621456 | tf_op jit(solution)/shard_map/all_gather | solution.py:98
  41.0 16.3 %fusion = (f32[1024,2,5]{0,2,1:T(8,128)S(1)}, f32[2,896,1024,5]{2,1,3,0:T(8,128)}) fusion(pred[1024,896]{0,1:T(8,128)(4,1)S(1)} %bitcast_compare_fusion, bf16[896,2,128,1]{0,2,3,1:T(8,128)(2,1)S(1)} %bitcast.144, bf16[1024,2,5,128]{0,3,2,1:T(8,128)(2,1)} %bitcast.138), kind=kOutput, calls=%fused_computation.2 | convolution fusion | flops 2376325120 | bytes 40738816 | tf_op jit(solution)/shard_map/tgrd,kgd->tgrk/dot_general | solution.py:39
  58.6 4.0 all-to-all-start
  64.9 15.7 %fusion.4 = f32[1024,2,5]{0,2,1:T(8,128)S(1)} fusion(f32[2,896,1024,5]{2,1,3,0:T(8,128)} %get-tuple-element.20, f32[1024,896]{0,1:T(8,128)S(1)} %bitcast.133, f32[1024,2,5]{0,2,1:T(8,128)S(1)} %get-tuple-element.14, pred[1024,896]{0,1:T(8,128)(4,1)S(1)} %bitcast_compare_fusion), kind=kLoop, calls=%fused_computation.6 | loop fusion | flops 45864960 | bytes 41369600 | tf_op jit(solution)/shard_map/reduce_sum | solution.py:47
  81.2 4.8 all-to-all-start.2
  86.1 17.6 %bitcast_add_fusion = f32[1024,2,5,128]{3,0,2,1:T(8,128)S(1)} fusion(f32[1024,2,5]{0,2,1:T(8,128)} %get-tuple-element.13, bf16[896,2,128,1]{0,2,3,1:T(8,128)(2,1)S(1)} %bitcast.150, f32[2,896,1024,5]{2,1,3,0:T(8,128)} %get-tuple-element.20, f32[1024,896]{0,1:T(8,128)} %bitcast.134, f32[1024,2,5]{0,2,1:T(8,128)S(1)} %get-tuple-element.14, ...), kind=kOutput, calls=%fused_computation.21 | convolution fusion | flops 2395996160 | bytes 47071232 | tf_op jit(solution)/shard_map/tgrk,kgd->tgrd/dot_general | solution.py:48
  106.4 17.0 %all-to-all-start.1 = ((f32[8,128,2,5,128]{4,1,3,2,0:T(8,128)}), f32[8,128,2,5,128]{4,1,3,2,0:T(8,128)}, u32[]{:S(2)}, u32[]{:S(2)}) async-start(f32[8,128,2,5,128]{4,1,3,2,0:T(8,128)} %copy.185), calls=%async_computation.1 | async-start | bytes 10485760 | tf_op jit(solution)/shard_map/all_to_all | solution.py:135
  143.4 4.1 collective-permute-start.9
  150.4 4.1 collective-permute-start.11
  157.5 4.1 collective-permute-start.13
  165.3 7.3 %collective-permute-done.14 = bf16[128,512]{0,1:T(8,128)(2,1)S(1)} collective-permute-done((bf16[128,512]{0,1:T(8,128)(2,1)S(1)}, bf16[128,512]{0,1:T(8,128)(2,1)S(1)}, u32[]{:S(2)}, u32[]{:S(2)}) %collective-permute-start.14) | collective-permute-done | bytes 131104 | tf_op jit(solution)/shard_map/ppermute | solution.py:26
  173.7 5.8 %fusion.9 = (f32[128,2,5]{0,2,1:T(8,128)S(1)}, f32[2,2048,128,5]{2,1,3,0:T(8,128)}) fusion(pred[128,2048]{0,1:T(8,128)(4,1)S(1)} %get-tuple-element.17, bf16[2048,2,128,1]{0,2,3,1:T(8,128)(2,1)S(1)} %bitcast.141, bf16[128,2,5,128]{0,3,2,1:T(8,128)(2,1)S(1)} %bitcast.140), kind=kOutput, calls=%fused_computation.14 | convolution fusion | flops 678951680 | bytes 12129280 | tf_op jit(solution)/shard_map/tgrd,kgd->tgrk/dot_general | solution.py:39
  179.7 6.4 %fusion.13 = f32[128,2,5]{0,2,1:T(8,128)S(1)} fusion(f32[2,2048,128,5]{2,1,3,0:T(8,128)} %get-tuple-element.22, f32[128,2048]{0,1:T(8,128)S(1)} %get-tuple-element.18, f32[128,2,5]{0,2,1:T(8,128)S(1)} %copy.188, pred[128,2048]{0,1:T(8,128)(4,1)S(1)} %get-tuple-element.17), kind=kLoop, calls=%fused_computation.18 | loop fusion | flops 13105920 | bytes 11806720 | tf_op jit(solution)/shard_map/reduce_sum | solution.py:47
  186.2 4.3 multiply_reduce_fusion
  192.7 7.9 %fusion.42 = bf16[128,2,5,128]{0,3,2,1:T(8,128)(2,1)S(1)} fusion(bf16[2048,2,128,1]{0,2,3,1:T(8,128)(2,1)} %bitcast.147, f32[2,2048,128,5]{2,1,3,0:T(8,128)} %get-tuple-element.22, f32[128,2048]{0,1:T(8,128)} %copy-done.4, f32[128,2,5]{0,2,1:T(8,128)S(1)} %copy.188, pred[128,2048]{0,1:T(8,128)(4,1)S(1)} %get-tuple-element.17, ...), kind=kOutput, calls=%fused_computation.49 | convolution fusion | flops 684851200 | bytes 13843456 | tf_op jit(solution)/shard_map/tgrk,kgd->tgrd/dot_general | solution.py:48
  205.2 134.4 %all_to_all.25 = bf16[128,16,2560]{2,1,0:T(8,128)(2,1)S(1)} all-to-all(bf16[128,16,2560]{2,1,0:T(8,128)(2,1)S(1)} %bitcast.130), channel_id=1, replica_groups=mesh['req'=8,'exp'=16] {'req','exp'}, dimensions={0} | all-to-all | bytes 20971520 | tf_op jit(solution)/shard_map/all_to_all | solution.py:196
  339.6 3.8 copy-done.2
  343.4 10.2 %fusion.21 = f32[2048,768]{1,0:T(8,128)} fusion(bf16[2048,2560]{1,0:T(8,128)(2,1)S(1)} %bitcast.136, bf16[1,2560,768]{2,1,0:T(8,128)(2,1)S(1)} %copy-done.10), kind=kOutput, calls=%fused_computation.27 | convolution fusion | flops 8053063680 | bytes 20709376 | tf_op jit(solution)/shard_map/dot_general | solution.py:199
  353.6 28.9 %convolution_convert_fusion = bf16[2048,2560]{1,0:T(8,128)(2,1)} fusion(f32[2048,768]{1,0:T(8,128)} %fusion.21, bf16[2048,2560]{1,0:T(8,128)(2,1)} %bitcast.137, bf16[1,768,2560]{2,1,0:T(8,128)(2,1)} %param.23, bf16[1,2560,768]{2,1,0:T(8,128)(2,1)} %param.22), kind=kOutput, calls=%fused_computation.10 | convolution fusion | flops 16120807424 | bytes 35127296 | tf_op jit(solution)/shard_map/dot_general | solution.py:203
  382.5 6.8 %all-to-all-start.4 = ((bf16[128,16,2560]{2,1,0:T(8,128)(2,1)}), bf16[128,16,2560]{2,1,0:T(8,128)(2,1)}, u32[]{:S(2)}, u32[]{:S(2)}) async-start(bf16[128,16,2560]{2,1,0:T(8,128)(2,1)} %bitcast.135), calls=%async_computation.4 | async-start | bytes 20971520 | tf_op jit(solution)/shard_map/all_to_all | solution.py:202
  390.2 141.3 %all-to-all-done.4 = bf16[128,16,2560]{2,1,0:T(8,128)(2,1)} async-done(((bf16[128,16,2560]{2,1,0:T(8,128)(2,1)}), bf16[128,16,2560]{2,1,0:T(8,128)(2,1)}, u32[]{:S(2)}, u32[]{:S(2)}) %all-to-all-start.4) | async-done | bytes 10485792 | tf_op jit(solution)/shard_map/all_to_all | solution.py:202
  531.5 5.6 %fusion.70 = f32[128,2560]{1,0:T(8,128)S(1)} fusion(bf16[128,2048]{0,1:T(8,128)(2,1)S(1)} %bitcast.143, bf16[2048,2560]{1,0:T(8,128)(2,1)} %bitcast.34), kind=kOutput, calls=%fused_computation.117 | convolution fusion | flops 1342177280 | bytes 12320768 | tf_op jit(solution)/shard_map/dot_general | solution.py:219
  537.2 6.4 %fusion.24 = bf16[128,2560]{1,0:T(8,128)(2,1)} fusion(f32[128,2560]{1,0:T(8,128)S(1)} %fusion.70, bf16[128,2048]{0,1:T(8,128)(2,1)S(1)} %bitcast.142, bf16[2048,2560]{1,0:T(8,128)(2,1)} %bitcast.34, bf16[128,2560]{1,0:T(8,128)(2,1)S(1)} %fusion.25), kind=kOutput, calls=%fused_computation.32 | convolution fusion | flops 1343488000 | bytes 13631488 | tf_op jit(solution)/shard_map/dot_general | solution.py:219
  (129 shorter events, 55.8 us)
Async XLA Ops:
  6.5 382.8 %copy-start = (bf16[2560,64]{0,1:T(8,128)(2,1)S(1)}, bf16[2560,64]{0,1:T(8,128)(2,1)}, u32[]{:S(2)}) copy-start(bf16[2560,64]{0,1:T(8,128)(2,1)} %param.19) | copy-start | bytes 983044
  6.5 34.5 %all-gather.2.cloned.1.call-start = ((), (), s32[]{:S(2)}) async-start(), calls=%async_computation.5 | async-start | bytes 2949120 | tf_op jit(solution)/shard_map/all_gather | solution.py:98
  9.5 114.6 %collective-permute-start = (bf16[128,512]{0,1:T(8,128)(2,1)S(1)}, bf16[128,512]{0,1:T(8,128)(2,1)}, u32[]{:S(2)}, u32[]{:S(2)}) collective-permute-start(bf16[128,512]{0,1:T(8,128)(2,1)S(1)} %copy.171), channel_id=1, source_target_pairs={{0,1},{1,2},{2,3},{3,4},{4,5},{5,6},{6,7},{7,8},{8,9},{9,10},{10,1... | collective-permute-start | bytes 393224 | tf_op jit(solution)/shard_map/ppermute | solution.py:26
  11.1 114.6 %collective-permute-start.1 = (bf16[128,512]{0,1:T(8,128)(2,1)S(1)}, bf16[128,512]{0,1:T(8,128)(2,1)}, u32[]{:S(2)}, u32[]{:S(2)}) collective-permute-start(bf16[128,512]{0,1:T(8,128)(2,1)S(1)} %copy.171), channel_id=1, source_target_pairs={{0,15},{1,0},{2,1},{3,2},{4,3},{5,4},{6,5},{7,6},{8,7},{9,8},{10,9... | collective-permute-start | bytes 393224 | tf_op jit(solution)/shard_map/ppermute | solution.py:31
  29.6 150.1 %copy-start.4 = (f32[128,2048]{0,1:T(8,128)}, f32[128,2048]{0,1:T(8,128)S(1)}, u32[]{:S(2)}) copy-start(f32[128,2048]{0,1:T(8,128)S(1)} %get-tuple-element.18) | copy-start | bytes 3145732
  58.6 22.6 %all-to-all-start = ((f32[8,128,2,5]{1,2,3,0:T(2,128)}), f32[8,128,2,5]{1,2,3,0:T(2,128)S(1)}, u32[]{:S(2)}, u32[]{:S(2)}) async-start(f32[8,128,2,5]{1,2,3,0:T(2,128)} %copy.169), calls=%async_computation | async-start | bytes 81920 | tf_op jit(solution)/shard_map/all_to_all | solution.py:121
  81.2 25.2 %all-to-all-start.2 = ((f32[8,128,2,5]{1,2,3,0:T(2,128)}), f32[8,128,2,5]{1,2,3,0:T(2,128)S(1)}, u32[]{:S(2)}, u32[]{:S(2)}) async-start(f32[8,128,2,5]{1,2,3,0:T(2,128)} %copy.191), calls=%async_computation.2 | async-start | bytes 81920 | tf_op jit(solution)/shard_map/all_to_all | solution.py:128
  106.4 79.7 %all-to-all-start.1 = ((f32[8,128,2,5,128]{4,1,3,2,0:T(8,128)}), f32[8,128,2,5,128]{4,1,3,2,0:T(8,128)}, u32[]{:S(2)}, u32[]{:S(2)}) async-start(f32[8,128,2,5,128]{4,1,3,2,0:T(8,128)} %copy.185), calls=%async_computation.1 | async-start | bytes 10485760 | tf_op jit(solution)/shard_map/all_to_all | solution.py:135
  123.9 49.9 %copy-start.3 = (bf16[128,1280]{0,1:T(8,128)(2,1)S(1)}, bf16[128,1280]{0,1:T(8,128)(2,1)}, u32[]{:S(2)}) copy-start(bf16[128,1280]{0,1:T(8,128)(2,1)} %copy.165) | copy-start | bytes 983044
  124.2 6.2 %collective-permute-start.2 = (bf16[128,512]{0,1:T(8,128)(2,1)}, bf16[128,512]{0,1:T(8,128)(2,1)S(1)}, u32[]{:S(2)}, u32[]{:S(2)}) collective-permute-start(bf16[128,512]{0,1:T(8,128)(2,1)} %collective-permute-done), channel_id=1, source_target_pairs={{0,1},{1,2},{2,3},{3,4},{4,5},{5,6},{6,7},{7,8},{8,9},{9,10},{10,1... | collective-permute-start | bytes 393224 | tf_op jit(solution)/shard_map/ppermute | solution.py:26
  125.7 6.1 %collective-permute-start.3 = (bf16[128,512]{0,1:T(8,128)(2,1)}, bf16[128,512]{0,1:T(8,128)(2,1)S(1)}, u32[]{:S(2)}, u32[]{:S(2)}) collective-permute-start(bf16[128,512]{0,1:T(8,128)(2,1)} %collective-permute-done.1), channel_id=1, source_target_pairs={{0,15},{1,0},{2,1},{3,2},{4,3},{5,4},{6,5},{7,6},{8,7},{9,8},{10,9... | collective-permute-start | bytes 393224 | tf_op jit(solution)/shard_map/ppermute | solution.py:31
  130.3 6.2 %collective-permute-start.4 = (bf16[128,512]{0,1:T(8,128)(2,1)S(1)}, bf16[128,512]{0,1:T(8,128)(2,1)S(1)}, u32[]{:S(2)}, u32[]{:S(2)}) collective-permute-start(bf16[128,512]{0,1:T(8,128)(2,1)S(1)} %collective-permute-done.2), channel_id=1, source_target_pairs={{0,1},{1,2},{2,3},{3,4},{4,5},{5,6},{6,7},{7,8},{8,9},{9,10},{10,1... | collective-permute-start | bytes 393224 | tf_op jit(solution)/shard_map/ppermute | solution.py:26
  131.8 5.2 collective-permute-start.5
  136.6 6.8 %collective-permute-start.6 = (bf16[128,512]{0,1:T(8,128)(2,1)S(1)}, bf16[128,512]{0,1:T(8,128)(2,1)S(1)}, u32[]{:S(2)}, u32[]{:S(2)}) collective-permute-start(bf16[128,512]{0,1:T(8,128)(2,1)S(1)} %collective-permute-done.4), channel_id=1, source_target_pairs={{0,1},{1,2},{2,3},{3,4},{4,5},{5,6},{6,7},{7,8},{8,9},{9,10},{10,1... | collective-permute-start | bytes 393224 | tf_op jit(solution)/shard_map/ppermute | solution.py:26
  137.0 6.3 %collective-permute-start.7 = (bf16[128,512]{0,1:T(8,128)(2,1)S(1)}, bf16[128,512]{0,1:T(8,128)(2,1)S(1)}, u32[]{:S(2)}, u32[]{:S(2)}) collective-permute-start(bf16[128,512]{0,1:T(8,128)(2,1)S(1)} %collective-permute-done.5), channel_id=1, source_target_pairs={{0,15},{1,0},{2,1},{3,2},{4,3},{5,4},{6,5},{7,6},{8,7},{9,8},{10,9... | collective-permute-start | bytes 393224 | tf_op jit(solution)/shard_map/ppermute | solution.py:31
  143.3 7.1 %collective-permute-start.8 = (bf16[128,512]{0,1:T(8,128)(2,1)S(1)}, bf16[128,512]{0,1:T(8,128)(2,1)S(1)}, u32[]{:S(2)}, u32[]{:S(2)}) collective-permute-start(bf16[128,512]{0,1:T(8,128)(2,1)S(1)} %collective-permute-done.6), channel_id=1, source_target_pairs={{0,1},{1,2},{2,3},{3,4},{4,5},{5,6},{6,7},{7,8},{8,9},{9,10},{10,1... | collective-permute-start | bytes 393224 | tf_op jit(solution)/shard_map/ppermute | solution.py:26
  143.4 7.1 %collective-permute-start.9 = (bf16[128,512]{0,1:T(8,128)(2,1)S(1)}, bf16[128,512]{0,1:T(8,128)(2,1)S(1)}, u32[]{:S(2)}, u32[]{:S(2)}) collective-permute-start(bf16[128,512]{0,1:T(8,128)(2,1)S(1)} %collective-permute-done.7), channel_id=1, source_target_pairs={{0,15},{1,0},{2,1},{3,2},{4,3},{5,4},{6,5},{7,6},{8,7},{9,8},{10,9... | collective-permute-start | bytes 393224 | tf_op jit(solution)/shard_map/ppermute | solution.py:31
  150.4 7.1 %collective-permute-start.10 = (bf16[128,512]{0,1:T(8,128)(2,1)S(1)}, bf16[128,512]{0,1:T(8,128)(2,1)S(1)}, u32[]{:S(2)}, u32[]{:S(2)}) collective-permute-start(bf16[128,512]{0,1:T(8,128)(2,1)S(1)} %collective-permute-done.8), channel_id=1, source_target_pairs={{0,1},{1,2},{2,3},{3,4},{4,5},{5,6},{6,7},{7,8},{8,9},{9,10},{10,1... | collective-permute-start | bytes 393224 | tf_op jit(solution)/shard_map/ppermute | solution.py:26
  150.4 7.1 %collective-permute-start.11 = (bf16[128,512]{0,1:T(8,128)(2,1)S(1)}, bf16[128,512]{0,1:T(8,128)(2,1)S(1)}, u32[]{:S(2)}, u32[]{:S(2)}) collective-permute-start(bf16[128,512]{0,1:T(8,128)(2,1)S(1)} %collective-permute-done.9), channel_id=1, source_target_pairs={{0,15},{1,0},{2,1},{3,2},{4,3},{5,4},{6,5},{7,6},{8,7},{9,8},{10,9... | collective-permute-start | bytes 393224 | tf_op jit(solution)/shard_map/ppermute | solution.py:31
  157.5 7.7 %collective-permute-start.12 = (bf16[128,512]{0,1:T(8,128)(2,1)S(1)}, bf16[128,512]{0,1:T(8,128)(2,1)S(1)}, u32[]{:S(2)}, u32[]{:S(2)}) collective-permute-start(bf16[128,512]{0,1:T(8,128)(2,1)S(1)} %collective-permute-done.10), channel_id=1, source_target_pairs={{0,1},{1,2},{2,3},{3,4},{4,5},{5,6},{6,7},{7,8},{8,9},{9,10},{10,1... | collective-permute-start | bytes 393224 | tf_op jit(solution)/shard_map/ppermute | solution.py:26
  157.5 7.7 %collective-permute-start.13 = (bf16[128,512]{0,1:T(8,128)(2,1)S(1)}, bf16[128,512]{0,1:T(8,128)(2,1)S(1)}, u32[]{:S(2)}, u32[]{:S(2)}) collective-permute-start(bf16[128,512]{0,1:T(8,128)(2,1)S(1)} %collective-permute-done.11), channel_id=1, source_target_pairs={{0,15},{1,0},{2,1},{3,2},{4,3},{5,4},{6,5},{7,6},{8,7},{9,8},{10,9... | collective-permute-start | bytes 393224 | tf_op jit(solution)/shard_map/ppermute | solution.py:31
  165.2 7.4 %collective-permute-start.14 = (bf16[128,512]{0,1:T(8,128)(2,1)S(1)}, bf16[128,512]{0,1:T(8,128)(2,1)S(1)}, u32[]{:S(2)}, u32[]{:S(2)}) collective-permute-start(bf16[128,512]{0,1:T(8,128)(2,1)S(1)} %collective-permute-done.12), channel_id=1, source_target_pairs={{0,1},{1,2},{2,3},{3,4},{4,5},{5,6},{6,7},{7,8},{8,9},{9,10},{10,1... | collective-permute-start | bytes 393224 | tf_op jit(solution)/shard_map/ppermute | solution.py:26
  205.2 138.2 %copy-start.10 = (bf16[1,2560,768]{2,1,0:T(8,128)(2,1)S(1)}, bf16[1,2560,768]{2,1,0:T(8,128)(2,1)}, u32[]{:S(2)}) copy-start(bf16[1,2560,768]{2,1,0:T(8,128)(2,1)} %param.21) | copy-start | bytes 11796484
  382.5 148.9 %all-to-all-start.4 = ((bf16[128,16,2560]{2,1,0:T(8,128)(2,1)}), bf16[128,16,2560]{2,1,0:T(8,128)(2,1)}, u32[]{:S(2)}, u32[]{:S(2)}) async-start(bf16[128,16,2560]{2,1,0:T(8,128)(2,1)} %bitcast.135), calls=%async_computation.4 | async-start | bytes 20971520 | tf_op jit(solution)/shard_map/all_to_all | solution.py:202
  (10 other events, 115.3 us)
Sparse Core Ops, SparseCore 0:
  9.0 31.9 all-gather.1
